TPU v7x, 256 devices: a whole 4x4x8 slice. The times are simulated.
256 devices in a mesh: dp: 128 (over x, y_lo, z, core), section: 2 (over y_hi).
Axes of the slice: x: 4, y: 4 (y_hi: 2, y_lo: 2; y = y_hi * 2 + y_lo), z: 8, core: 2. Of those that a mesh axis runs over, the one named last changes fastest.
Arguments:
- replay_rows: bfloat16 [65536, 4, 4, 128], P('dp'), may hold values from -6 to 6
- qvalues: bfloat16 [65536, 18], P('dp'), may hold values from -5 to 129
- target_logits: bfloat16 [65536, 18], P('dp'), may hold values from -8 to 258
- replay_owner: int32 [32768], P(('dp', 'section')), may hold values from 0 to 127, as said below
- replay_slot: int32 [32768], P(('dp', 'section')), may hold values from 0 to 511
- sample_actions: int32 [32768, 20], P(('dp', 'section')), may hold values from 0 to 17
- weights: bfloat16 [2, 147456], replicated, may hold values from -0.1875 to 0.1875
- head: bfloat16 [128, 18], replicated, may hold values from -0.5 to 0.5
- master: float32 [2, 147456], P('section', 'dp'), may hold values from -0.0012 to 0.0012
- moment_first: float32 [2, 147456], P('section', 'dp'), may hold values from -0.0021 to 0.0021
- moment_second: float32 [2, 147456], P('section', 'dp'), may hold values from 9.9e-14 to 1.01e-06
Outputs:
- adam_step: float32 [2, 147456], P('section', 'dp')
- new_weights: bfloat16 [2, 147456], replicated
Inputs may be any that keep to these rules, and one draw needn't show every extreme that they name: `replay_owner`: among the 128 rows of one learner device no shard is named more than 2 times; in every draw one shard is named exactly 2 times by every learner device.
All inputs are finite; a program needn't handle non-finite values.
Results may differ from a plain program's by a relative error of at most 0.013.
Values may be sent and summed in bfloat16 or wider, within the bound.
No kernel may reach another device: no remote copies, remote signals or barrier semaphores. Data moves between devices by JAX's collectives and lax.ppermute only.
A program may use at most 192 MiB of HBM per device.

v0:
```python
import jax
import jax.numpy as jnp
from jax import lax
from jax.sharding import PartitionSpec as P

constant_entropy_scale = 0.5
trust_weight = 0.5
beta_first = 0.9
beta_second = 0.999
epsilon = 1e-08
learn_rate = 0.0001


def tap_stack(field):
    grid_side = field.shape[1]
    padded_rows = jnp.pad(field, ((0, 0), (1, 1), (1, 1), (0, 0)))
    return jnp.concatenate(
        [
            padded_rows[:, shift_row : shift_row + grid_side, shift_col : shift_col + grid_side, :]
            for shift_row in range(3)
            for shift_col in range(3)
        ],
        axis=-1,
    )


def layer_grads(
    features,
    move_return_estimates,
    reference_policy_entries,
    actions,
    row_scale,
    w_first,
    second_weight,
    head,
):
    row_count, grid_side, _, channels = features.shape
    positions = row_count * grid_side * grid_side
    taps_first = tap_stack(features).reshape(positions, 9 * channels)
    hidden = jax.nn.relu(jnp.dot(taps_first, w_first, preferred_element_type=jnp.float32)).astype(
        jnp.bfloat16
    )
    taps_second = tap_stack(hidden.reshape(features.shape)).reshape(positions, 9 * channels)
    summed = features.reshape(positions, channels).astype(jnp.float32) + jnp.dot(
        taps_second, second_weight, preferred_element_type=jnp.float32
    )
    block_out = jax.nn.relu(summed).astype(jnp.bfloat16)
    averaged_embedding = jnp.mean(
        block_out.astype(jnp.float32).reshape(row_count, grid_side * grid_side, channels), axis=1
    ).astype(jnp.bfloat16)
    logits = reference_policy_entries.astype(jnp.float32) + jnp.dot(
        averaged_embedding, head, preferred_element_type=jnp.float32
    )
    policy = jax.nn.softmax(logits, axis=-1)
    prior = jax.nn.softmax(reference_policy_entries.astype(jnp.float32), axis=-1)
    selected_moves = (actions[:, :, None] == jnp.arange(head.shape[1])[None, None, :]).astype(
        jnp.float32
    )
    move_logit_matrix = (
        jnp.einsum("vlu,vu->vl", selected_moves, move_return_estimates.astype(jnp.float32))
        / constant_entropy_scale
    )
    sample_weight = jax.nn.softmax(move_logit_matrix, axis=-1)
    logit_grad = (
        (1.0 + trust_weight) * policy
        - jnp.einsum("nk,nka->na", sample_weight, selected_moves)
        - trust_weight * prior
    ) * row_scale[:, None]
    pooled_grad = jnp.dot(logit_grad, head.astype(jnp.float32).T, precision=lax.Precision.HIGHEST)
    spread = jnp.broadcast_to(
        (pooled_grad / (grid_side * grid_side))[:, None, :],
        (row_count, grid_side * grid_side, channels),
    ).reshape(positions, channels)
    out_grad = jnp.where(block_out > 0, spread, 0.0).astype(jnp.bfloat16)
    grad_second = lax.dot_general(
        taps_second, out_grad, (((0,), (0,)), ((), ())), preferred_element_type=jnp.float32
    )
    flipped = (
        second_weight.reshape(9, channels, channels)[::-1]
        .transpose(0, 2, 1)
        .reshape(9 * channels, channels)
    )
    taps_back = tap_stack(out_grad.reshape(features.shape)).reshape(positions, 9 * channels)
    hidden_grad = jnp.where(
        hidden > 0, jnp.dot(taps_back, flipped, preferred_element_type=jnp.float32), 0.0
    ).astype(jnp.bfloat16)
    grad_first = lax.dot_general(
        taps_first, hidden_grad, (((0,), (0,)), ((), ())), preferred_element_type=jnp.float32
    )
    return (grad_first, grad_second)


def per_device(
    replay_rows,
    qvalues,
    target_logits,
    replay_owner,
    replay_slot,
    sample_actions,
    weights,
    head,
    master,
    moment_first,
    moment_second,
):
    rows_dev = replay_owner.shape[0]
    owners = lax.axis_size("dp")
    capacity = 2 * rows_dev // owners
    learn_rows = rows_dev * owners * lax.axis_size("section")
    channels = replay_rows.shape[3]
    w_first = weights[0].reshape(9 * channels, channels)
    second_weight = weights[1].reshape(9 * channels, channels)
    row_order = jnp.arange(rows_dev, dtype=jnp.int32)
    earlier = (replay_owner[None, :] == replay_owner[:, None]) & (
        row_order[None, :] < row_order[:, None]
    )
    rank_within = jnp.sum(earlier.astype(jnp.int32), axis=1)
    slot_index = replay_owner * capacity + rank_within
    matches = slot_index[None, :] == jnp.arange(owners * capacity, dtype=jnp.int32)[:, None]
    occupied_entries = jnp.any(matches, axis=1)
    source = jnp.sum(jnp.where(matches, row_order[None, :], 0), axis=1)
    request = jnp.where(occupied_entries, jnp.take(replay_slot, source), -1).reshape(
        owners, capacity
    )
    row_index = jnp.maximum(
        lax.all_to_all(request, "dp", split_axis=0, concat_axis=0, tiled=True), 0
    )
    feature_slots = lax.all_to_all(
        jnp.take(replay_rows, row_index, axis=0), "dp", split_axis=0, concat_axis=0, tiled=True
    )
    qvalue_slots = lax.all_to_all(
        jnp.take(qvalues, row_index, axis=0), "dp", split_axis=0, concat_axis=0, tiled=True
    )
    prior_slots = lax.all_to_all(
        jnp.take(target_logits, row_index, axis=0), "dp", split_axis=0, concat_axis=0, tiled=True
    )
    features = jnp.take(
        feature_slots.reshape((owners * capacity,) + feature_slots.shape[2:]), slot_index, axis=0
    )
    move_return_estimates = jnp.take(
        qvalue_slots.reshape(owners * capacity, -1), slot_index, axis=0
    )
    reference_policy_entries = jnp.take(
        prior_slots.reshape(owners * capacity, -1), slot_index, axis=0
    )
    row_scale = jnp.full((rows_dev,), 1.0 / learn_rows, jnp.float32)
    grad_first, grad_second = layer_grads(
        features,
        move_return_estimates,
        reference_policy_entries,
        sample_actions,
        row_scale,
        w_first,
        second_weight,
        head,
    )
    loss_derivative = jnp.stack([grad_first.reshape(-1), grad_second.reshape(-1)])
    piece_len = loss_derivative.shape[1] // owners
    regrouped = (
        loss_derivative.reshape(2, owners, piece_len)
        .transpose(1, 0, 2)
        .reshape(2 * owners, piece_len)
    )
    owned_grad = lax.psum_scatter(regrouped, ("dp", "section"), scatter_dimension=0, tiled=True)
    first = beta_first * moment_first + (1.0 - beta_first) * owned_grad
    second = beta_second * moment_second + (1.0 - beta_second) * owned_grad * owned_grad
    adam_step = first / (jnp.sqrt(second) + epsilon)
    new_piece = (master - learn_rate * adam_step).astype(jnp.bfloat16)
    collected = lax.all_gather(new_piece, ("dp", "section"), axis=0, tiled=True)
    new_weights = (
        collected.reshape(owners, 2, piece_len).transpose(1, 0, 2).reshape(2, owners * piece_len)
    )
    return (adam_step, new_weights)


def solution(mesh):
    placed = (
        P("dp", None, None, None),
        P("dp", None),
        P("dp", None),
        P(("dp", "section")),
        P(("dp", "section")),
        P(("dp", "section"), None),
        P(),
        P(),
        P("section", "dp"),
        P("section", "dp"),
        P("section", "dp"),
    )
    return jax.shard_map(
        per_device, mesh=mesh, in_specs=placed, out_specs=(P("section", "dp"), P()), check_vma=False
    )
```

profile of v0, /device:TPU:0, one launch (start us, length us, event | category | flops | bytes accessed | tf_op | source)
XLA Modules:
  0.0 1061.6 jit_solution(8042441142103392493)
XLA Ops:
  7.2 1.0 convert_reduce_fusion.1
  8.2 0.7 compare_and_fusion.1
  9.1 0.2 reduce_or.12
  9.2 0.1 reduce_sum.60
  9.4 1.9 gather_fusion
  11.3 0.1 gather.23
  11.5 0.7 select_select_fusion
  12.1 12.5 %all-to-all-start = ((s32[128,1,2]{2,1,0:T(1,128)}), s32[128,1,2]{2,1,0:T(1,128)S(1)}, u32[]{:S(2)}, u32[]{:S(2)}) async-start(s32[128,1,2]{2,1,0:T(1,128)} %bitcast.3), calls=%async_computation | async-start | bytes 131072 | tf_op jit(solution)/shard_map/all_to_all | solution.py:126
  24.6 0.9 copy.39
  25.5 0.9 copy.41
  26.4 8.6 all-to-all-done
  35.1 0.1 reshape.285
  35.2 0.1 reshape.259
  35.4 0.9 gather_fusion.3
  36.2 0.9 gather_fusion.5
  37.1 0.9 broadcast_select_fusion.3
  37.9 6.2 all-to-all-start.3
  44.1 1.5 gather_fusion.1
  45.7 8.9 all-to-all-done.3
  54.6 6.1 all-to-all-start.2
  60.7 1.5 broadcast_select_fusion
  62.3 8.9 all-to-all-done.2
  71.1 6.2 all-to-all-start.1
  77.4 0.2 broadcast_in_dim.103
  77.6 0.2 broadcast_in_dim.104
  77.8 8.4 slice_reduce_fusion
  86.2 0.7 copy-done.3
  87.0 0.8 reverse_bitcast_fusion
  87.7 1.8 copy.42
  89.6 0.7 gather_fusion.6
  90.5 0.7 gather_fusion.4
  91.5 14.9 %all-to-all-done.1 = bf16[128,2,4,4,128]{4,3,2,1,0:T(4,128)(2,1)S(1)} async-done(((bf16[128,2,4,4,128]{4,3,2,1,0:T(4,128)(2,1)}), bf16[128,2,4,4,128]{4,3,2,1,0:T(4,128)(2,1)S(1)}, u32[]{:S(2)}, u32[]{:S(2)}) %all-to-all-start.1) | async-done | bytes 1048608 | tf_op jit(solution)/shard_map/all_to_all | solution.py:128
  106.4 1.0 copy-done.1
  107.4 2.3 gather_fusion.2
  109.7 0.3 broadcast_select_fusion.1
  110.0 1.1 fusion.6
  111.1 1.1 fusion.7
  112.3 1.1 fusion.8
  113.4 1.2 fusion.9
  114.6 1.2 constant_dynamic-update-slice_fusion
  115.8 1.2 fusion.10
  116.9 1.1 fusion.11
  118.1 1.1 fusion.12
  119.2 1.1 fusion.13
  120.3 8.5 reshape.203
  128.9 3.7 fusion.2
  132.6 1.7 pad_slice_fusion.8
  135.5 1.9 convert_reduce_fusion
  137.5 0.1 fusion.52
  137.6 0.3 convolution_multiply_fusion
  137.9 0.2 fusion.4
  138.1 2.3 fusion.53
  140.4 1.2 stack.8
  141.5 1.8 pad_slice_fusion
  144.5 2.2 copy-done.7
  146.7 8.8 fusion.5
  155.5 1.2 stack.7
  156.8 0.9 copy.43
  157.7 1.9 reshape.212
  159.6 258.0 %all-reduce.6.cloned.1.call-done = f32[256,1152]{1,0:T(8,128)} async-done(((f32[256,1152]{1,0:T(8,128)}), f32[256,1152]{1,0:T(8,128)}) %all-reduce.6.cloned.1.call-update) | async-done | bytes 1179664
  417.6 1.4 convert_bitcast_fusion
  419.0 628.6 %all-gather = bf16[256,1,1152]{2,1,0:T(2,128)(2,1)S(1)} all-gather(bf16[1,1,1152]{2,1,0:T(2,128)(2,1)S(1)} %get-tuple-element.6), channel_id=1, replica_groups=mesh['dp'=128,'section'=2] {'dp','section'}, dimensions={0}, use_global_device_ids=true | all-gather | bytes 592128 | tf_op jit(solution)/shard_map/all_gather | solution.py:169
  1047.6 4.4 reduce.6
  1052.0 2.6 reshape.213
  (66 shorter events, 3.2 us)
Async XLA Ops:
  7.2 37.0 %copy-start = (bf16[512,4,4,128]{3,2,1,0:T(4,128)(2,1)S(1)}, bf16[512,4,4,128]{3,2,1,0:T(4,128)(2,1)}, u32[]{:S(2)}) copy-start(bf16[512,4,4,128]{3,2,1,0:T(4,128)(2,1)} %param.15) | copy-start | bytes 6291460
  12.1 22.9 %all-to-all-start = ((s32[128,1,2]{2,1,0:T(1,128)}), s32[128,1,2]{2,1,0:T(1,128)S(1)}, u32[]{:S(2)}, u32[]{:S(2)}) async-start(s32[128,1,2]{2,1,0:T(1,128)} %bitcast.3), calls=%async_computation | async-start | bytes 131072 | tf_op jit(solution)/shard_map/all_to_all | solution.py:126
  37.9 16.6 %all-to-all-start.3 = ((bf16[128,2,18]{2,1,0:T(2,128)(2,1)}), bf16[128,2,18]{2,1,0:T(2,128)(2,1)S(1)}, u32[]{:S(2)}, u32[]{:S(2)}) async-start(bf16[128,2,18]{2,1,0:T(2,128)(2,1)} %get-tuple-element.29), calls=%async_computation.3 | async-start | bytes 131072 | tf_op jit(solution)/shard_map/all_to_all | solution.py:131
  44.1 47.2 %copy-start.8 = (s32[128,20]{0,1:T(8,128)S(1)}, s32[128,20]{0,1:T(8,128)}, u32[]{:S(2)}) copy-start(s32[128,20]{0,1:T(8,128)} %param.20) | copy-start | bytes 30724
  54.6 16.6 %all-to-all-start.2 = ((bf16[128,2,18]{2,1,0:T(2,128)(2,1)}), bf16[128,2,18]{2,1,0:T(2,128)(2,1)S(1)}, u32[]{:S(2)}, u32[]{:S(2)}) async-start(bf16[128,2,18]{2,1,0:T(2,128)(2,1)} %get-tuple-element.28), calls=%async_computation.2 | async-start | bytes 131072 | tf_op jit(solution)/shard_map/all_to_all | solution.py:134
  71.1 35.3 %all-to-all-start.1 = ((bf16[128,2,4,4,128]{4,3,2,1,0:T(4,128)(2,1)}), bf16[128,2,4,4,128]{4,3,2,1,0:T(4,128)(2,1)S(1)}, u32[]{:S(2)}, u32[]{:S(2)}) async-start(bf16[128,2,4,4,128]{4,3,2,1,0:T(4,128)(2,1)} %broadcast_select_fusion), calls=%async_computation.1 | async-start | bytes 2097152 | tf_op jit(solution)/shard_map/all_to_all | solution.py:128
  77.3 340.2 %all-reduce.6.cloned.1.call-start = ((), (), s32[]{:S(2)}) async-start(), calls=%async_computation.4 | async-start | bytes 2359296
  86.2 0.7 copy-start.3
  106.4 1.0 copy-start.1
  120.3 8.5 copy-start.5
  132.6 2.4 copy-start.2
  134.3 1.2 copy-start.4
  135.5 1.9 copy-start.9
  143.3 3.4 copy-start.6
  144.5 2.2 copy-start.7
  155.5 262.1 %copy-start.10 = (f32[1,1152]{1,0:T(1,128)S(1)}, f32[1,1152]{1,0:T(1,128)}, u32[]{:S(2)}) copy-start(f32[1,1152]{1,0:T(1,128)} %param.23) | copy-start | bytes 13828
  155.5 262.1 %copy-start.11 = (f32[1,1152]{1,0:T(1,128)S(1)}, f32[1,1152]{1,0:T(1,128)}, u32[]{:S(2)}) copy-start(f32[1,1152]{1,0:T(1,128)} %param.25) | copy-start | bytes 13828
  155.5 262.1 %copy-start.12 = (f32[1,1152]{1,0:T(1,128)S(1)}, f32[1,1152]{1,0:T(1,128)}, u32[]{:S(2)}) copy-start(f32[1,1152]{1,0:T(1,128)} %param.24) | copy-start | bytes 13828
Sparse Core Ops, SparseCore 0:
  159.7 257.8 all-reduce.5
where the time goes:
time: 1070 us; the launch traced here: 1060 us
  blocking collectives  629 us (59%)
  waiting for transfers between devices  299 us (28%)
  local copies, waits for them, and re-layouts  57.9 us (5%)
  starting transfers between devices  31 us (3%)
  matrix products  17.1 us (2%)
  between operations  14.8 us (1%)
  other arithmetic  12.8 us (1%)
    all_gather x1, blocking collectives, per_device(): collected = lax.all_gather(new_piece, ('dp', 'section'), axis=0, tiled=True)  629 us
    unnamed x2, waiting for transfers between devices  258 us
  transfers between devices with their start and end apart: 5, of which 5 were waited for; matrix products, arithmetic and copies ran while one was open for 2% of the time, Pallas kernels for 0%

commit v1 on v0

--- a/solution.py
+++ b/solution.py
@@ -166,7 +166,12 @@
     second = beta_second * moment_second + (1.0 - beta_second) * owned_grad * owned_grad
     adam_step = first / (jnp.sqrt(second) + epsilon)
     new_piece = (master - learn_rate * adam_step).astype(jnp.bfloat16)
-    collected = lax.all_gather(new_piece, ("dp", "section"), axis=0, tiled=True)
+    collected = jnp.concatenate(
+        lax.all_to_all(
+            jnp.stack([new_piece] * lax.axis_size(("dp", "section"))), ("dp", "section"), 0, 0
+        ),
+        axis=0,
+    )
     new_weights = (
         collected.reshape(owners, 2, piece_len).transpose(1, 0, 2).reshape(2, owners * piece_len)
     )

time: 1070 us -> 491 us (0.46)
  the two profiles are of different devices: /device:TPU:0 before, /device:TPU:1 now
where the time goes in v1:
time: 491 us; the launch traced here: 482 us
  waiting for transfers between devices  298 us (61%)
  local copies, waits for them, and re-layouts  66 us (13%)
  blocking collectives  34.4 us (7%)
  starting transfers between devices  32.2 us (7%)
  other arithmetic  19 us (4%)
  matrix products  17.2 us (4%)
  between operations  15 us (3%)
    unnamed x2, waiting for transfers between devices  254 us
    all_to_all x1, blocking collectives, per_device(): lax.all_to_all(jnp.stack([new_piece] * lax.axis_size(('dp', 'section'))),...  34.4 us
    unnamed x54, local copies, waits for them, and re-layouts  22.1 us
    all_to_all x1, waiting for transfers between devices, per_device(): lax.all_to_all(jnp.take(replay_rows, row_index, axis=0), 'dp', split_axis...  16.6 us
    all_to_all x1, starting transfers between devices, per_device(): lax.all_to_all(request, 'dp', split_axis=0, concat_axis=0, tiled=True)  14.8 us
  transfers between devices with their start and end apart: 5, of which 5 were waited for; matrix products, arithmetic and copies ran while one was open for 4% of the time, Pallas kernels for 0%

profile of v1, /device:TPU:1, one launch (start us, length us, event | category | flops | bytes accessed | tf_op | source)
XLA Modules:
  0.0 481.7 jit_solution(2882919465159461653)
XLA Ops:
  7.2 1.0 convert_reduce_fusion.1
  8.2 0.7 compare_and_fusion.1
  9.4 1.9 gather_fusion
  11.5 0.7 select_select_fusion
  12.1 14.8 %all-to-all-start = ((s32[128,1,2]{2,1,0:T(1,128)}), s32[128,1,2]{2,1,0:T(1,128)S(1)}, u32[]{:S(2)}, u32[]{:S(2)}) async-start(s32[128,1,2]{2,1,0:T(1,128)} %bitcast.3), calls=%async_computation | async-start | bytes 131072 | tf_op jit(solution)/shard_map/all_to_all | solution.py:126
  26.9 0.9 copy.39
  27.8 0.9 copy.41
  28.7 8.9 %all-to-all-done = s32[128,1,2]{2,1,0:T(1,128)S(1)} async-done(((s32[128,1,2]{2,1,0:T(1,128)}), s32[128,1,2]{2,1,0:T(1,128)S(1)}, u32[]{:S(2)}, u32[]{:S(2)}) %all-to-all-start) | async-done | bytes 1056 | tf_op jit(solution)/shard_map/all_to_all | solution.py:126
  37.9 0.9 gather_fusion.3
  38.8 0.9 gather_fusion.5
  39.6 0.9 broadcast_select_fusion.3
  40.5 5.8 %all-to-all-start.3 = ((bf16[128,2,18]{2,1,0:T(2,128)(2,1)}), bf16[128,2,18]{2,1,0:T(2,128)(2,1)S(1)}, u32[]{:S(2)}, u32[]{:S(2)}) async-start(bf16[128,2,18]{2,1,0:T(2,128)(2,1)} %get-tuple-element.29), calls=%async_computation.3 | async-start | bytes 131072 | tf_op jit(solution)/shard_map/all_to_all | solution.py:131
  46.3 1.5 gather_fusion.1
  47.9 9.3 %all-to-all-done.3 = bf16[128,2,18]{2,1,0:T(2,128)(2,1)S(1)} async-done(((bf16[128,2,18]{2,1,0:T(2,128)(2,1)}), bf16[128,2,18]{2,1,0:T(2,128)(2,1)S(1)}, u32[]{:S(2)}, u32[]{:S(2)}) %all-to-all-start.3) | async-done | bytes 9248 | tf_op jit(solution)/shard_map/all_to_all | solution.py:131
  57.2 5.8 %all-to-all-start.2 = ((bf16[128,2,18]{2,1,0:T(2,128)(2,1)}), bf16[128,2,18]{2,1,0:T(2,128)(2,1)S(1)}, u32[]{:S(2)}, u32[]{:S(2)}) async-start(bf16[128,2,18]{2,1,0:T(2,128)(2,1)} %get-tuple-element.28), calls=%async_computation.2 | async-start | bytes 131072 | tf_op jit(solution)/shard_map/all_to_all | solution.py:134
  62.9 1.5 broadcast_select_fusion
  64.5 9.3 %all-to-all-done.2 = bf16[128,2,18]{2,1,0:T(2,128)(2,1)S(1)} async-done(((bf16[128,2,18]{2,1,0:T(2,128)(2,1)}), bf16[128,2,18]{2,1,0:T(2,128)(2,1)S(1)}, u32[]{:S(2)}, u32[]{:S(2)}) %all-to-all-start.2) | async-done | bytes 9248 | tf_op jit(solution)/shard_map/all_to_all | solution.py:134
  73.7 5.8 %all-to-all-start.1 = ((bf16[128,2,4,4,128]{4,3,2,1,0:T(4,128)(2,1)}), bf16[128,2,4,4,128]{4,3,2,1,0:T(4,128)(2,1)S(1)}, u32[]{:S(2)}, u32[]{:S(2)}) async-start(bf16[128,2,4,4,128]{4,3,2,1,0:T(4,128)(2,1)} %broadcast_select_fusion), calls=%async_computation.1 | async-start | bytes 2097152 | tf_op jit(solution)/shard_map/all_to_all | solution.py:128
  79.6 0.2 broadcast_in_dim.103
  79.8 0.2 broadcast_in_dim.104
  80.0 8.1 %slice_reduce_fusion = (bf16[147456]{0:T(1024)(128)(2,1)S(1)}, bf16[147456]{0:T(1024)(128)(2,1)}) fusion(bf16[2,147456]{1,0:T(2,128)(2,1)} %param.21), kind=kLoop, calls=%fused_computation.46 | loop fusion | bytes 1179648 | tf_op jit(solution)/shard_map/slice | solution.py:112
  88.1 0.7 copy-done.3
  88.9 0.8 reverse_bitcast_fusion
  89.6 1.8 copy.42
  91.5 0.7 gather_fusion.6
  92.4 0.7 gather_fusion.4
  93.4 16.6 %all-to-all-done.1 = bf16[128,2,4,4,128]{4,3,2,1,0:T(4,128)(2,1)S(1)} async-done(((bf16[128,2,4,4,128]{4,3,2,1,0:T(4,128)(2,1)}), bf16[128,2,4,4,128]{4,3,2,1,0:T(4,128)(2,1)S(1)}, u32[]{:S(2)}, u32[]{:S(2)}) %all-to-all-start.1) | async-done | bytes 1048608 | tf_op jit(solution)/shard_map/all_to_all | solution.py:128
  110.0 1.0 copy-done.1
  111.0 2.3 gather_fusion.2
  113.3 0.3 broadcast_select_fusion.1
  113.6 1.1 fusion.6
  114.7 1.1 fusion.7
  115.9 1.1 fusion.8
  117.0 1.2 fusion.9
  118.2 1.2 constant_dynamic-update-slice_fusion
  119.4 1.2 fusion.10
  120.5 1.1 fusion.11
  121.7 1.1 fusion.12
  122.8 1.1 fusion.13
  123.9 8.5 %reshape.203 = bf16[2048,1152]{1,0:T(8,128)(2,1)} reshape(bf16[128,4,4,1152]{3,2,1,0:T(4,128)(2,1)} %fusion.13) | data formatting | bytes 9437184 | tf_op jit(solution)/shard_map/reshape | solution.py:39
  132.5 3.7 fusion.2
  136.2 1.7 pad_slice_fusion.8
  139.1 1.9 convert_reduce_fusion
  141.3 0.3 convolution_multiply_fusion
  141.6 0.2 fusion.4
  141.8 2.3 fusion.53
  144.0 1.2 stack.9
  145.2 1.8 pad_slice_fusion
  148.1 2.2 copy-done.7
  150.3 8.8 %fusion.5 = f32[1152,128]{1,0:T(8,128)} fusion(bf16[2048,1152]{1,0:T(8,128)(2,1)} %reshape.203, bf16[2048,1152]{1,0:T(8,128)(2,1)} %copy-done.7, bf16[1152,128]{1,0:T(8,128)(2,1)S(1)} %bitcast.101, bf16[2048,128]{1,0:T(8,128)(2,1)} %copy-done.2), kind=kOutput, calls=%fused_computation.45 | convolution fusion | flops 1208745984 | bytes 10846208 | tf_op jit(solution)/shard_map/dot_general | solution.py:87
  159.1 2.0 stack.8
  161.1 1.1 maximum_bitcast_fusion
  162.3 0.9 copy.43
  163.2 1.9 reshape.212
  165.1 253.9 %all-reduce.6.cloned.1.call-done = f32[256,1152]{1,0:T(8,128)} async-done(((f32[256,1152]{1,0:T(8,128)}), f32[256,1152]{1,0:T(8,128)}) %all-reduce.6.cloned.1.call-update) | async-done | bytes 1179664
  419.0 1.4 convert_reduce_fusion.2
  420.4 0.6 stack.11
  421.0 0.6 broadcast.181
  421.6 5.1 %reduce.13 = bf16[256,1152]{1,0:T(8,128)(2,1)} reduce(bf16[256,1,1152]{2,1,0:T(2,128)(2,1)S(1)} %stack.11, bf16[]{:T(256)} %broadcast.181), dimensions={1}, to_apply=%stack.11.reduce_sub_computation | reduce | bytes 1179650 | tf_op jit(solution)/shard_map/stack | solution.py:171
  426.7 2.2 reshape.302
  428.9 34.4 %all_to_all.26 = bf16[256,2,576]{2,1,0:T(2,128)(2,1)} all-to-all(bf16[256,2,576]{2,1,0:T(2,128)(2,1)S(1)} %reshape.302), channel_id=1, replica_groups=mesh['dp'=128,'section'=2] {'dp','section'}, dimensions={0} | all-to-all | bytes 1179648 | tf_op jit(solution)/shard_map/all_to_all | solution.py:170
  463.3 4.2 reshape.303
  467.5 4.4 reduce.7
  471.9 2.6 reshape_reshape.3
  (71 shorter events, 4.0 us)
Async XLA Ops:
  7.2 39.1 %copy-start = (bf16[512,4,4,128]{3,2,1,0:T(4,128)(2,1)S(1)}, bf16[512,4,4,128]{3,2,1,0:T(4,128)(2,1)}, u32[]{:S(2)}) copy-start(bf16[512,4,4,128]{3,2,1,0:T(4,128)(2,1)} %param.15) | copy-start | bytes 6291460
  12.1 25.4 %all-to-all-start = ((s32[128,1,2]{2,1,0:T(1,128)}), s32[128,1,2]{2,1,0:T(1,128)S(1)}, u32[]{:S(2)}, u32[]{:S(2)}) async-start(s32[128,1,2]{2,1,0:T(1,128)} %bitcast.3), calls=%async_computation | async-start | bytes 131072 | tf_op jit(solution)/shard_map/all_to_all | solution.py:126
  40.5 16.6 %all-to-all-start.3 = ((bf16[128,2,18]{2,1,0:T(2,128)(2,1)}), bf16[128,2,18]{2,1,0:T(2,128)(2,1)S(1)}, u32[]{:S(2)}, u32[]{:S(2)}) async-start(bf16[128,2,18]{2,1,0:T(2,128)(2,1)} %get-tuple-element.29), calls=%async_computation.3 | async-start | bytes 131072 | tf_op jit(solution)/shard_map/all_to_all | solution.py:131
  46.3 46.9 %copy-start.8 = (s32[128,20]{0,1:T(8,128)S(1)}, s32[128,20]{0,1:T(8,128)}, u32[]{:S(2)}) copy-start(s32[128,20]{0,1:T(8,128)} %param.20) | copy-start | bytes 30724
  57.2 16.6 %all-to-all-start.2 = ((bf16[128,2,18]{2,1,0:T(2,128)(2,1)}), bf16[128,2,18]{2,1,0:T(2,128)(2,1)S(1)}, u32[]{:S(2)}, u32[]{:S(2)}) async-start(bf16[128,2,18]{2,1,0:T(2,128)(2,1)} %get-tuple-element.28), calls=%async_computation.2 | async-start | bytes 131072 | tf_op jit(solution)/shard_map/all_to_all | solution.py:134
  73.7 36.3 %all-to-all-start.1 = ((bf16[128,2,4,4,128]{4,3,2,1,0:T(4,128)(2,1)}), bf16[128,2,4,4,128]{4,3,2,1,0:T(4,128)(2,1)S(1)}, u32[]{:S(2)}, u32[]{:S(2)}) async-start(bf16[128,2,4,4,128]{4,3,2,1,0:T(4,128)(2,1)} %broadcast_select_fusion), calls=%async_computation.1 | async-start | bytes 2097152 | tf_op jit(solution)/shard_map/all_to_all | solution.py:128
  79.5 339.5 %all-reduce.6.cloned.1.call-start = ((), (), s32[]{:S(2)}) async-start(), calls=%async_computation.5 | async-start | bytes 2359296
  88.1 0.7 copy-start.3
  110.0 1.0 copy-start.1
  123.9 8.5 %copy-start.5 = (bf16[147456]{0:T(1024)(128)(2,1)S(1)}, bf16[147456]{0:T(1024)(128)(2,1)}, u32[]{:S(2)}) copy-start(bf16[147456]{0:T(1024)(128)(2,1)} %get-tuple-element.5) | copy-start | bytes 884740
  136.2 2.4 copy-start.2
  137.9 1.2 copy-start.4
  139.1 2.0 copy-start.9
  146.9 3.4 copy-start.6
  148.1 2.2 copy-start.7
  159.1 259.9 %copy-start.10 = (f32[1,1152]{1,0:T(1,128)S(1)}, f32[1,1152]{1,0:T(1,128)}, u32[]{:S(2)}) copy-start(f32[1,1152]{1,0:T(1,128)} %param.23) | copy-start | bytes 13828
  159.1 259.9 %copy-start.11 = (f32[1,1152]{1,0:T(1,128)S(1)}, f32[1,1152]{1,0:T(1,128)}, u32[]{:S(2)}) copy-start(f32[1,1152]{1,0:T(1,128)} %param.25) | copy-start | bytes 13828
  159.1 259.9 %copy-start.12 = (f32[1,1152]{1,0:T(1,128)S(1)}, f32[1,1152]{1,0:T(1,128)}, u32[]{:S(2)}) copy-start(f32[1,1152]{1,0:T(1,128)} %param.24) | copy-start | bytes 13828
Sparse Core Ops, SparseCore 0:
  165.2 253.7 all-reduce.5
